TPU v7x, 32 devices: a whole 2x2x4 slice. The times are simulated.
32 devices in a mesh: gx: 4 (over x, core), gy: 8 (over z, y).
Axes of the slice: x: 2, y: 2, z: 4, core: 2. Of those that a mesh axis runs over, the one named last changes fastest.
Arguments:
- c_upper: bfloat16 [4, 8, 96, 96], P('gx', 'gy'), may hold values from -60 to 60
- edge_upper: bfloat16 [4, 8, 96, 1536], P('gx', 'gy'), may hold values from -60 to 60
- edge_left: bfloat16 [4, 8, 96, 1536], P('gx', 'gy'), may hold values from -60 to 60
- c_lower: bfloat16 [4, 8, 96, 96], P('gx', 'gy'), may hold values from -60 to 60
- edge_lower: bfloat16 [4, 8, 96, 1536], P('gx', 'gy'), may hold values from -60 to 60
- site_ket: bfloat16 [4, 8, 2, 256], P('gx', 'gy'), may hold values from -6 to 6
- time_gate: float32 [2, 2], replicated, may hold values from -3 to 3
- quench_sites: int32 [4], replicated, may hold values from 0 to 31
Outputs:
- new_c_upper: bfloat16 [4, 8, 96, 96], P('gx', 'gy')
- new_edge_left: bfloat16 [4, 8, 96, 1536], P('gx', 'gy')
- new_c_lower: bfloat16 [4, 8, 96, 96], P('gx', 'gy')
All inputs are finite; a program needn't handle non-finite values.
Results may differ from a plain program's by a relative error of at most 0.03.
Values may be sent and summed in bfloat16 or wider, within the bound.
No kernel may reach another device: no remote copies, remote signals or barrier semaphores. Data moves between devices by JAX's collectives and lax.ppermute only.
A program may use at most 64 MiB of HBM per device.

v0:
```python
import math

import jax
import jax.numpy as jnp
from jax import lax
from jax.sharding import PartitionSpec as P

NS_ITERS = 6
STEPS = 2


def passed_along(shard, axis, by):
    peers = lax.axis_size(axis)
    return lax.ppermute(shard, axis, [(i, (i + by) % peers) for i in range(peers)])


def polar_factor(matrix):
    scale = jnp.sqrt(jnp.sum(matrix * matrix) + 1e-06)
    iterate = matrix / scale
    for sweep in range(NS_ITERS):
        gram = jnp.dot(iterate.T, iterate, precision=lax.Precision.HIGHEST)
        iterate = 1.5 * iterate - 0.5 * jnp.dot(iterate, gram, precision=lax.Precision.HIGHEST)
    return iterate


def unit_scaled(tensor):
    return tensor / jnp.sqrt(jnp.mean(tensor * tensor) + 1e-06)


def per_device(
    c_upper, edge_upper, edge_left, c_lower, edge_lower, site_ket, time_gate, quench_sites
):
    env_width = c_upper.shape[-1]
    double_bond = edge_upper.shape[-1] // env_width
    bond_dim = math.isqrt(double_bond)
    phys_dim = site_ket.shape[2]
    ket_sites = site_ket[0, 0].reshape(phys_dim, bond_dim, bond_dim, bond_dim, bond_dim)
    gram = jnp.dot(time_gate.T, time_gate, precision=lax.Precision.HIGHEST)
    gated = jnp.einsum(
        "st,tabcd->sabcd", gram, ket_sites.astype(jnp.float32), precision=lax.Precision.HIGHEST
    )
    own_index = lax.axis_index("gx") * lax.axis_size("gy") + lax.axis_index("gy")
    chosen = jnp.any(quench_sites == own_index)
    bra = jnp.where(chosen, gated, ket_sites.astype(jnp.float32)).astype(jnp.bfloat16)
    north_edge = edge_upper[0, 0]
    south_edge = edge_lower[0, 0]
    corner_up = c_upper[0, 0]
    west_edge = edge_left[0, 0]
    corner_low = c_lower[0, 0]
    block = math.gcd(env_width, 16)
    starts = jnp.arange(env_width // block, dtype=jnp.int32) * block
    for step in range(STEPS):
        upper = jnp.dot(corner_up, north_edge, preferred_element_type=jnp.float32).reshape(
            env_width * double_bond, env_width
        )
        lower = jnp.dot(corner_low, south_edge, preferred_element_type=jnp.float32).reshape(
            env_width * double_bond, env_width
        )
        from_below = passed_along(upper.astype(jnp.bfloat16), "gy", -1).astype(upper.dtype)
        proj_below = polar_factor(lower + from_below)
        proj_above = passed_along(proj_below.astype(jnp.bfloat16), "gy", 1).astype(proj_below.dtype)
        low_half = proj_below.astype(jnp.bfloat16).reshape(env_width, double_bond, env_width)
        up_half = proj_above.astype(jnp.bfloat16).reshape(env_width, bond_dim, bond_dim, env_width)
        west = west_edge.reshape(env_width, double_bond, env_width)

        def one_block(start):
            columns = lax.dynamic_slice_in_dim(low_half, start, block, 2)
            first = jnp.einsum(
                "ulw,wdj->uldj", west, columns, preferred_element_type=jnp.float32
            ).astype(jnp.bfloat16)
            first = first.reshape(env_width, bond_dim, bond_dim, bond_dim, bond_dim, block)
            second = jnp.einsum(
                "uaebfj,sagcb->uefjsgc", first, ket_sites, preferred_element_type=jnp.float32
            ).astype(jnp.bfloat16)
            third = jnp.einsum(
                "uefjsgc,sehkf->ughckj", second, bra, preferred_element_type=jnp.float32
            ).astype(jnp.bfloat16)
            return jnp.einsum(
                "ughi,ughckj->jick", up_half, third, preferred_element_type=jnp.float32
            )

        pieces = lax.map(one_block, starts)
        edge_new = pieces.reshape(env_width, env_width, bond_dim, bond_dim)
        edge_new = jnp.transpose(edge_new, (1, 2, 3, 0)).reshape(env_width, double_bond * env_width)
        edge_new = unit_scaled(edge_new).astype(jnp.bfloat16)
        new_up = jnp.dot(proj_above.T, upper, precision=lax.Precision.HIGHEST)
        new_low = jnp.dot(proj_below.T, lower, precision=lax.Precision.HIGHEST)
        new_up = unit_scaled(new_up).astype(jnp.bfloat16)
        new_low = unit_scaled(new_low).astype(jnp.bfloat16)
        corner_up, west_edge, corner_low = passed_along((new_up, edge_new, new_low), "gx", 1)
    return (corner_up[None, None], west_edge[None, None], corner_low[None, None])


def solution(mesh):
    return jax.shard_map(
        per_device,
        mesh=mesh,
        in_specs=(
            P("gx", "gy", None, None),
            P("gx", "gy", None, None),
            P("gx", "gy", None, None),
            P("gx", "gy", None, None),
            P("gx", "gy", None, None),
            P("gx", "gy", None, None),
            P(),
            P(),
        ),
        out_specs=(P("gx", "gy", None, None), P("gx", "gy", None, None), P("gx", "gy", None, None)),
        check_vma=False,
    )
```

profile of v0, /device:TPU:0, one launch (start us, length us, event | category | flops | bytes accessed | tf_op | source)
XLA Modules:
  0.0 183.0 jit_solution(392538066823902406)
XLA Ops:
  0.7 0.9 copy-done
  1.6 0.9 fusion.53
  3.0 6.1 %collective-permute-start = (bf16[1536,96]{0,1:T(8,128)(2,1)S(1)}, bf16[1536,96]{0,1:T(8,128)(2,1)S(1)}, u32[]{:S(2)}, u32[]{:S(2)}) collective-permute-start(bf16[1536,96]{0,1:T(8,128)(2,1)S(1)} %copy.49), channel_id=1, source_target_pairs={{0,7},{1,0},{2,1},{3,2},{4,3},{5,4},{6,5},{7,6},{8,15},{9,8},{10,9... | collective-permute-start | bytes 884744 | tf_op jit(solution)/shard_map/ppermute | solution.py:14
  10.8 0.9 fusion.46
  11.7 3.6 %collective-permute-done = bf16[1536,96]{0,1:T(8,128)(2,1)S(1)} collective-permute-done((bf16[1536,96]{0,1:T(8,128)(2,1)S(1)}, bf16[1536,96]{0,1:T(8,128)(2,1)S(1)}, u32[]{:S(2)}, u32[]{:S(2)}) %collective-permute-start) | collective-permute-done | bytes 294944 | tf_op jit(solution)/shard_map/ppermute | solution.py:14
  24.3 1.4 fusion.68
  27.8 1.2 copy.54
  29.0 1.9 %multiply_reduce_fusion.7 = (f32[]{:T(128)}, f32[96,96]{1,0:T(8,128)}) fusion(f32[1536,96]{0,1:T(8,128)S(1)} %get-tuple-element.172, f32[1536,96]{1,0:T(8,128)S(1)} %reshape.57), kind=kOutput, calls=%fused_computation.92 | convolution fusion | flops 169887744 | bytes 1216516 | tf_op jit(solution)/shard_map/dot_general | solution.py:87
  32.0 5.4 %collective-permute-done.2 = bf16[1536,96]{0,1:T(8,128)(2,1)} collective-permute-done((bf16[1536,96]{0,1:T(8,128)(2,1)}, bf16[1536,96]{0,1:T(8,128)(2,1)}, u32[]{:S(2)}, u32[]{:S(2)}) %collective-permute-start.2) | collective-permute-done | bytes 294944 | tf_op jit(solution)/shard_map/ppermute | solution.py:14
  37.4 2.0 %multiply_reduce_fusion.6 = (f32[]{:T(128)}, f32[96,96]{1,0:T(8,128)S(1)}) fusion(bf16[1536,96]{0,1:T(8,128)(2,1)} %collective-permute-done.2, f32[1536,96]{1,0:T(8,128)S(1)} %reshape.58), kind=kOutput, calls=%fused_computation.90 | convolution fusion | flops 169887744 | bytes 921604 | tf_op jit(solution)/shard_map/dot_general | solution.py:86
  40.4 1.2 copy.57
  41.8 46.4 %while.20 = (s32[]{:T(128)}, f32[6,16,96,4,4]{2,1,4,3,0:T(8,128)S(1)}, s32[6]{0:T(128)S(1)}, bf16[96,16,96]{0,2,1:T(8,128)(2,1)S(1)}, bf16[96,16,96]{2,0,1:T(8,1...) while((s32[]{:T(128)}, ...), condition=%wide.region_7.8_spmd, body=%wide.region_6.7_spmd.sunk | while | flops 202899456 | bytes 7538859 | solution.py:82
  44.8 1.8 fusion.165
  46.6 2.0 %fusion.166 = bf16[96,4,4,4,4,16]{0,4,2,3,1,5:T(4,128)(2,1)S(1)} fusion(bf16[96,4,4,16,2,4,4,1]{0,6,5,4,3,2,1,7:T(4,128)(2,1)S(1)} %fusion.165, bf16[2,4,4,4,4]{4,3,0,1,2:T(4,128)(2,1)S(1)} %get-tuple-element.307), kind=kOutput, calls=%fused_computation.6.clone.1 | convolution fusion | flops 25559040 | bytes 2360320 | tf_op jit(solution)/shard_map/while/body/eval_jaxpr/uefjsgc,sehkf->ughckj/dot_general | solution.py:75
  48.7 0.9 fusion.167
  52.6 1.8 fusion.165
  54.4 2.0 %fusion.166 = bf16[96,4,4,4,4,16]{0,4,2,3,1,5:T(4,128)(2,1)S(1)} fusion(bf16[96,4,4,16,2,4,4,1]{0,6,5,4,3,2,1,7:T(4,128)(2,1)S(1)} %fusion.165, bf16[2,4,4,4,4]{4,3,0,1,2:T(4,128)(2,1)S(1)} %get-tuple-element.307), kind=kOutput, calls=%fused_computation.6.clone.1 | convolution fusion | flops 25559040 | bytes 2360320 | tf_op jit(solution)/shard_map/while/body/eval_jaxpr/uefjsgc,sehkf->ughckj/dot_general | solution.py:75
  56.4 0.9 fusion.167
  60.3 1.8 fusion.165
  62.1 2.0 %fusion.166 = bf16[96,4,4,4,4,16]{0,4,2,3,1,5:T(4,128)(2,1)S(1)} fusion(bf16[96,4,4,16,2,4,4,1]{0,6,5,4,3,2,1,7:T(4,128)(2,1)S(1)} %fusion.165, bf16[2,4,4,4,4]{4,3,0,1,2:T(4,128)(2,1)S(1)} %get-tuple-element.307), kind=kOutput, calls=%fused_computation.6.clone.1 | convolution fusion | flops 25559040 | bytes 2360320 | tf_op jit(solution)/shard_map/while/body/eval_jaxpr/uefjsgc,sehkf->ughckj/dot_general | solution.py:75
  64.1 0.9 fusion.167
  68.0 1.8 fusion.165
  69.8 2.0 %fusion.166 = bf16[96,4,4,4,4,16]{0,4,2,3,1,5:T(4,128)(2,1)S(1)} fusion(bf16[96,4,4,16,2,4,4,1]{0,6,5,4,3,2,1,7:T(4,128)(2,1)S(1)} %fusion.165, bf16[2,4,4,4,4]{4,3,0,1,2:T(4,128)(2,1)S(1)} %get-tuple-element.307), kind=kOutput, calls=%fused_computation.6.clone.1 | convolution fusion | flops 25559040 | bytes 2360320 | tf_op jit(solution)/shard_map/while/body/eval_jaxpr/uefjsgc,sehkf->ughckj/dot_general | solution.py:75
  71.9 0.9 fusion.167
  75.8 1.8 fusion.165
  77.6 2.0 %fusion.166 = bf16[96,4,4,4,4,16]{0,4,2,3,1,5:T(4,128)(2,1)S(1)} fusion(bf16[96,4,4,16,2,4,4,1]{0,6,5,4,3,2,1,7:T(4,128)(2,1)S(1)} %fusion.165, bf16[2,4,4,4,4]{4,3,0,1,2:T(4,128)(2,1)S(1)} %get-tuple-element.307), kind=kOutput, calls=%fused_computation.6.clone.1 | convolution fusion | flops 25559040 | bytes 2360320 | tf_op jit(solution)/shard_map/while/body/eval_jaxpr/uefjsgc,sehkf->ughckj/dot_general | solution.py:75
  79.6 0.9 fusion.167
  83.5 1.8 fusion.165
  85.3 2.0 %fusion.166 = bf16[96,4,4,4,4,16]{0,4,2,3,1,5:T(4,128)(2,1)S(1)} fusion(bf16[96,4,4,16,2,4,4,1]{0,6,5,4,3,2,1,7:T(4,128)(2,1)S(1)} %fusion.165, bf16[2,4,4,4,4]{4,3,0,1,2:T(4,128)(2,1)S(1)} %get-tuple-element.307), kind=kOutput, calls=%fused_computation.6.clone.1 | convolution fusion | flops 25559040 | bytes 2360320 | tf_op jit(solution)/shard_map/while/body/eval_jaxpr/uefjsgc,sehkf->ughckj/dot_general | solution.py:75
  87.4 0.9 fusion.167
  88.3 0.8 multiply_reduce_fusion.1
  90.0 1.7 collective-permute-start.7
  92.2 0.9 copy.51
  93.0 1.7 collective-permute-start.4
  94.9 3.2 %collective-permute-done.1 = bf16[96,96]{1,0:T(8,128)(2,1)S(1)} collective-permute-done((bf16[96,96]{1,0:T(8,128)(2,1)S(1)}, bf16[96,96]{1,0:T(8,128)(2,1)S(1)}, u32[]{:S(2)}, u32[]{:S(2)}) %collective-permute-start.1) | collective-permute-done | bytes 18464 | tf_op jit(solution)/shard_map/ppermute | solution.py:14
  98.9 1.3 reshape.64
  100.3 2.0 %collective-permute-done.4 = bf16[1536,96]{0,1:T(8,128)(2,1)} collective-permute-done((bf16[1536,96]{0,1:T(8,128)(2,1)}, bf16[1536,96]{0,1:T(8,128)(2,1)}, u32[]{:S(2)}, u32[]{:S(2)}) %collective-permute-start.4) | collective-permute-done | bytes 294944 | tf_op jit(solution)/shard_map/ppermute | solution.py:14
  102.3 1.7 multiply_reduce_fusion.2
  104.7 1.8 fusion.59
  106.5 1.8 %multiply_subtract_fusion = f32[1536,96]{0,1:T(8,128)S(1)} fusion(f32[96,96]{1,0:T(8,128)S(1)} %fusion.59, f32[]{:T(128)S(6)} %sqrt.27, f32[1536,96]{0,1:T(8,128)S(1)} %copy.52, bf16[1536,96]{0,1:T(8,128)(2,1)} %collective-permute-done.4), kind=kOutput, calls=%fused_computation.67 | convolution fusion | flops 171196416 | bytes 1511428 | tf_op jit(solution)/shard_map/dot_general | solution.py:22
  115.1 1.3 multiply_reduce_fusion.4
  118.1 7.8 %collective-permute-done.5 = bf16[1536,96]{0,1:T(8,128)(2,1)S(1)} collective-permute-done((bf16[1536,96]{0,1:T(8,128)(2,1)S(1)}, bf16[1536,96]{0,1:T(8,128)(2,1)S(1)}, u32[]{:S(2)}, u32[]{:S(2)}) %collective-permute-start.5) | collective-permute-done | bytes 294944 | tf_op jit(solution)/shard_map/ppermute | solution.py:14
  126.4 46.4 %while.21 = (s32[]{:T(128)}, f32[6,16,96,4,4]{2,1,4,3,0:T(8,128)S(1)}, s32[6]{0:T(128)S(1)}, bf16[96,16,96]{0,2,1:T(8,128)(2,1)S(1)}, bf16[96,16,96]{2,0,1:T(8,1...) while((s32[]{:T(128)}, ...), condition=%wide.region_10.11_spmd, body=%wide.region_9.10_spmd.sunk | while | flops 202899456 | bytes 7538859 | solution.py:82
  129.4 1.8 fusion.176
  131.2 2.0 %fusion.177 = bf16[96,4,4,4,4,16]{0,4,2,3,1,5:T(4,128)(2,1)S(1)} fusion(bf16[96,4,4,16,2,4,4,1]{0,6,5,4,3,2,1,7:T(4,128)(2,1)S(1)} %fusion.176, bf16[2,4,4,4,4]{4,3,0,1,2:T(4,128)(2,1)S(1)} %get-tuple-element.340), kind=kOutput, calls=%fused_computation.24.clone.1 | convolution fusion | flops 25559040 | bytes 2360320 | tf_op jit(solution)/shard_map/while/body/eval_jaxpr/uefjsgc,sehkf->ughckj/dot_general | solution.py:75
  133.2 0.9 fusion.178
  137.1 1.8 fusion.176
  138.9 2.0 %fusion.177 = bf16[96,4,4,4,4,16]{0,4,2,3,1,5:T(4,128)(2,1)S(1)} fusion(bf16[96,4,4,16,2,4,4,1]{0,6,5,4,3,2,1,7:T(4,128)(2,1)S(1)} %fusion.176, bf16[2,4,4,4,4]{4,3,0,1,2:T(4,128)(2,1)S(1)} %get-tuple-element.340), kind=kOutput, calls=%fused_computation.24.clone.1 | convolution fusion | flops 25559040 | bytes 2360320 | tf_op jit(solution)/shard_map/while/body/eval_jaxpr/uefjsgc,sehkf->ughckj/dot_general | solution.py:75
  141.0 0.9 fusion.178
  144.9 1.8 fusion.176
  146.7 2.0 %fusion.177 = bf16[96,4,4,4,4,16]{0,4,2,3,1,5:T(4,128)(2,1)S(1)} fusion(bf16[96,4,4,16,2,4,4,1]{0,6,5,4,3,2,1,7:T(4,128)(2,1)S(1)} %fusion.176, bf16[2,4,4,4,4]{4,3,0,1,2:T(4,128)(2,1)S(1)} %get-tuple-element.340), kind=kOutput, calls=%fused_computation.24.clone.1 | convolution fusion | flops 25559040 | bytes 2360320 | tf_op jit(solution)/shard_map/while/body/eval_jaxpr/uefjsgc,sehkf->ughckj/dot_general | solution.py:75
  148.7 0.9 fusion.178
  152.6 1.8 fusion.176
  154.4 2.0 %fusion.177 = bf16[96,4,4,4,4,16]{0,4,2,3,1,5:T(4,128)(2,1)S(1)} fusion(bf16[96,4,4,16,2,4,4,1]{0,6,5,4,3,2,1,7:T(4,128)(2,1)S(1)} %fusion.176, bf16[2,4,4,4,4]{4,3,0,1,2:T(4,128)(2,1)S(1)} %get-tuple-element.340), kind=kOutput, calls=%fused_computation.24.clone.1 | convolution fusion | flops 25559040 | bytes 2360320 | tf_op jit(solution)/shard_map/while/body/eval_jaxpr/uefjsgc,sehkf->ughckj/dot_general | solution.py:75
  156.4 0.9 fusion.178
  160.3 1.8 fusion.176
  162.1 2.0 %fusion.177 = bf16[96,4,4,4,4,16]{0,4,2,3,1,5:T(4,128)(2,1)S(1)} fusion(bf16[96,4,4,16,2,4,4,1]{0,6,5,4,3,2,1,7:T(4,128)(2,1)S(1)} %fusion.176, bf16[2,4,4,4,4]{4,3,0,1,2:T(4,128)(2,1)S(1)} %get-tuple-element.340), kind=kOutput, calls=%fused_computation.24.clone.1 | convolution fusion | flops 25559040 | bytes 2360320 | tf_op jit(solution)/shard_map/while/body/eval_jaxpr/uefjsgc,sehkf->ughckj/dot_general | solution.py:75
  164.2 0.9 fusion.178
  168.1 1.8 fusion.176
  169.9 2.0 %fusion.177 = bf16[96,4,4,4,4,16]{0,4,2,3,1,5:T(4,128)(2,1)S(1)} fusion(bf16[96,4,4,16,2,4,4,1]{0,6,5,4,3,2,1,7:T(4,128)(2,1)S(1)} %fusion.176, bf16[2,4,4,4,4]{4,3,0,1,2:T(4,128)(2,1)S(1)} %get-tuple-element.340), kind=kOutput, calls=%fused_computation.24.clone.1 | convolution fusion | flops 25559040 | bytes 2360320 | tf_op jit(solution)/shard_map/while/body/eval_jaxpr/uefjsgc,sehkf->ughckj/dot_general | solution.py:75
  171.9 0.9 fusion.178
  172.8 0.8 multiply_reduce_fusion
  174.6 1.1 multiply_reduce_fusion.5
  177.1 3.9 %collective-permute-done.6 = bf16[96,96]{1,0:T(8,128)(2,1)S(1)} collective-permute-done((bf16[96,96]{1,0:T(8,128)(2,1)S(1)}, bf16[96,96]{1,0:T(8,128)(2,1)S(1)}, u32[]{:S(2)}, u32[]{:S(2)}) %collective-permute-start.6) | collective-permute-done | bytes 18464 | tf_op jit(solution)/shard_map/ppermute | solution.py:14
  (118 shorter events, 38.4 us)
Async XLA Ops:
  0.6 1.0 copy-start
  0.6 8.4 %copy-start.10 = (f32[2,2]{1,0:T(2,128)S(1)}, f32[2,2]{1,0:T(2,128)}, u32[]{:S(2)}) copy-start(f32[2,2]{1,0:T(2,128)} %param.18) | copy-start | bytes 52
  0.7 8.6 %copy-start.9 = (bf16[1,1,2,256]{3,2,1,0:T(2,128)(2,1)S(1)}, bf16[1,1,2,256]{3,2,1,0:T(2,128)(2,1)}, u32[]{:S(2)}) copy-start(bf16[1,1,2,256]{3,2,1,0:T(2,128)(2,1)} %param.17) | copy-start | bytes 3076
  0.7 8.7 %copy-start.1 = (bf16[1,1,96,1536]{3,2,1,0:T(8,128)(2,1)S(1)}, bf16[1,1,96,1536]{3,2,1,0:T(8,128)(2,1)}, u32[]{:S(2)}) copy-start(bf16[1,1,96,1536]{3,2,1,0:T(8,128)(2,1)} %param.16) | copy-start | bytes 884740
  0.7 8.7 %copy-start.8 = (bf16[1,1,96,96]{3,2,1,0:T(8,128)(2,1)S(1)}, bf16[1,1,96,96]{3,2,1,0:T(8,128)(2,1)}, u32[]{:S(2)}) copy-start(bf16[1,1,96,96]{3,2,1,0:T(8,128)(2,1)} %param.15) | copy-start | bytes 55300
  3.0 7.2 %copy-start.11 = (s32[4]{0:T(128)S(1)}, s32[4]{0:T(128)}, u32[]{:S(2)}) copy-start(s32[4]{0:T(128)} %param.19) | copy-start | bytes 52
  3.0 12.4 %collective-permute-start = (bf16[1536,96]{0,1:T(8,128)(2,1)S(1)}, bf16[1536,96]{0,1:T(8,128)(2,1)S(1)}, u32[]{:S(2)}, u32[]{:S(2)}) collective-permute-start(bf16[1536,96]{0,1:T(8,128)(2,1)S(1)} %copy.49), channel_id=1, source_target_pairs={{0,7},{1,0},{2,1},{3,2},{4,3},{5,4},{6,5},{7,6},{8,15},{9,8},{10,9... | collective-permute-start | bytes 884744 | tf_op jit(solution)/shard_map/ppermute | solution.py:14
  23.0 4.4 %copy-start.2 = (bf16[1,1,96,1536]{3,2,1,0:T(8,128)(2,1)S(1)}, bf16[1,1,96,1536]{3,2,1,0:T(8,128)(2,1)}, u32[]{:S(2)}) copy-start(bf16[1,1,96,1536]{3,2,1,0:T(8,128)(2,1)} %param.14) | copy-start | bytes 884740
  25.8 11.6 %collective-permute-start.2 = (bf16[1536,96]{0,1:T(8,128)(2,1)}, bf16[1536,96]{0,1:T(8,128)(2,1)}, u32[]{:S(2)}, u32[]{:S(2)}) collective-permute-start(bf16[1536,96]{0,1:T(8,128)(2,1)} %get-tuple-element.171), channel_id=1, source_target_pairs={{0,1},{1,2},{2,3},{3,4},{4,5},{5,6},{6,7},{7,0},{8,9},{9,10},{10,1... | collective-permute-start | bytes 884744 | tf_op jit(solution)/shard_map/ppermute | solution.py:14
  31.6 10.1 %copy-start.4 = (bf16[2,4,4,4,4]{4,3,1,2,0:T(4,128)(2,1)S(1)}, bf16[2,4,4,4,4]{4,3,1,2,0:T(4,128)(2,1)}, u32[]{:S(2)}) copy-start(bf16[2,4,4,4,4]{4,3,1,2,0:T(4,128)(2,1)} %copy.60) | copy-start | bytes 3076
  31.6 10.1 %copy-start.6 = (bf16[2,4,4,4,4]{4,3,0,1,2:T(4,128)(2,1)S(1)}, bf16[2,4,4,4,4]{4,3,0,1,2:T(4,128)(2,1)}, u32[]{:S(2)}) copy-start(bf16[2,4,4,4,4]{4,3,0,1,2:T(4,128)(2,1)} %copy.61) | copy-start | bytes 3076
  40.2 51.5 %collective-permute-start.3 = (bf16[96,96]{1,0:T(8,128)(2,1)S(1)}, bf16[96,96]{1,0:T(8,128)(2,1)S(1)}, u32[]{:S(2)}, u32[]{:S(2)}) collective-permute-start(bf16[96,96]{1,0:T(8,128)(2,1)S(1)} %divide_convert_fusion.2), channel_id=1, source_target_pairs={{0,8},{8,16},{16,24},{24,0},{1,9},{9,17},{17,25},{25,1},{2,10},{10... | collective-permute-start | bytes 55304 | tf_op jit(solution)/shard_map/ppermute | solution.py:14
  89.8 5.0 %copy-start.3 = (f32[96,96]{1,0:T(8,128)S(1)}, f32[96,96]{1,0:T(8,128)}, u32[]{:S(2)}) copy-start(f32[96,96]{1,0:T(8,128)} %get-tuple-element.170) | copy-start | bytes 110596
  90.0 8.8 %collective-permute-start.7 = (bf16[96,1536]{1,0:T(8,128)(2,1)S(1)}, bf16[96,1536]{1,0:T(8,128)(2,1)}, u32[]{:S(2)}, u32[]{:S(2)}) collective-permute-start(bf16[96,1536]{1,0:T(8,128)(2,1)S(1)} %copy.100), channel_id=1, source_target_pairs={{0,8},{8,16},{16,24},{24,0},{1,9},{9,17},{17,25},{25,1},{2,10},{10... | collective-permute-start | bytes 884744 | tf_op jit(solution)/shard_map/ppermute | solution.py:14
  93.0 9.3 %collective-permute-start.4 = (bf16[1536,96]{0,1:T(8,128)(2,1)}, bf16[1536,96]{0,1:T(8,128)(2,1)}, u32[]{:S(2)}, u32[]{:S(2)}) collective-permute-start(bf16[1536,96]{0,1:T(8,128)(2,1)} %copy.51), channel_id=1, source_target_pairs={{0,7},{1,0},{2,1},{3,2},{4,3},{5,4},{6,5},{7,6},{8,15},{9,8},{10,9... | collective-permute-start | bytes 884744 | tf_op jit(solution)/shard_map/ppermute | solution.py:14
  94.8 3.3 %collective-permute-start.1 = (bf16[96,96]{1,0:T(8,128)(2,1)S(1)}, bf16[96,96]{1,0:T(8,128)(2,1)S(1)}, u32[]{:S(2)}, u32[]{:S(2)}) collective-permute-start(bf16[96,96]{1,0:T(8,128)(2,1)S(1)} %divide_convert_fusion.3), channel_id=1, source_target_pairs={{0,8},{8,16},{16,24},{24,0},{1,9},{9,17},{17,25},{25,1},{2,10},{10... | collective-permute-start | bytes 55304 | tf_op jit(solution)/shard_map/ppermute | solution.py:14
  115.1 10.8 %collective-permute-start.5 = (bf16[1536,96]{0,1:T(8,128)(2,1)S(1)}, bf16[1536,96]{0,1:T(8,128)(2,1)S(1)}, u32[]{:S(2)}, u32[]{:S(2)}) collective-permute-start(bf16[1536,96]{0,1:T(8,128)(2,1)S(1)} %get-tuple-element.175), channel_id=1, source_target_pairs={{0,1},{1,2},{2,3},{3,4},{4,5},{5,6},{6,7},{7,0},{8,9},{9,10},{10,1... | collective-permute-start | bytes 884744 | tf_op jit(solution)/shard_map/ppermute | solution.py:14
  116.5 9.9 %copy-start.5 = (bf16[2,4,4,4,4]{4,3,1,2,0:T(4,128)(2,1)S(1)}, bf16[2,4,4,4,4]{4,3,1,2,0:T(4,128)(2,1)}, u32[]{:S(2)}) copy-start(bf16[2,4,4,4,4]{4,3,1,2,0:T(4,128)(2,1)} %copy.60) | copy-start | bytes 3076
  116.5 9.9 %copy-start.7 = (bf16[2,4,4,4,4]{4,3,0,1,2:T(4,128)(2,1)S(1)}, bf16[2,4,4,4,4]{4,3,0,1,2:T(4,128)(2,1)}, u32[]{:S(2)}) copy-start(bf16[2,4,4,4,4]{4,3,0,1,2:T(4,128)(2,1)} %copy.61) | copy-start | bytes 3076
  117.4 59.7 %collective-permute-start.9 = (bf16[96,96]{1,0:T(8,128)(2,1)S(1)}, bf16[96,96]{1,0:T(8,128)(2,1)S(1)}, u32[]{:S(2)}, u32[]{:S(2)}) collective-permute-start(bf16[96,96]{1,0:T(8,128)(2,1)S(1)} %divide_convert_fusion), channel_id=1, source_target_pairs={{0,8},{8,16},{16,24},{24,0},{1,9},{9,17},{17,25},{25,1},{2,10},{10... | collective-permute-start | bytes 55304 | tf_op jit(solution)/shard_map/ppermute | solution.py:14
  174.6 6.5 %collective-permute-start.8 = (bf16[96,1536]{1,0:T(8,128)(2,1)S(1)}, bf16[96,1536]{1,0:T(8,128)(2,1)S(1)}, u32[]{:S(2)}, u32[]{:S(2)}) collective-permute-start(bf16[96,1536]{1,0:T(8,128)(2,1)S(1)} %copy.72), channel_id=1, source_target_pairs={{0,8},{8,16},{16,24},{24,0},{1,9},{9,17},{17,25},{25,1},{2,10},{10... | collective-permute-start | bytes 884744 | tf_op jit(solution)/shard_map/ppermute | solution.py:14
  176.4 4.6 %collective-permute-start.6 = (bf16[96,96]{1,0:T(8,128)(2,1)S(1)}, bf16[96,96]{1,0:T(8,128)(2,1)S(1)}, u32[]{:S(2)}, u32[]{:S(2)}) collective-permute-start(bf16[96,96]{1,0:T(8,128)(2,1)S(1)} %divide_convert_fusion.1), channel_id=1, source_target_pairs={{0,8},{8,16},{16,24},{24,0},{1,9},{9,17},{17,25},{25,1},{2,10},{10... | collective-permute-start | bytes 55304 | tf_op jit(solution)/shard_map/ppermute | solution.py:14
where the time goes:
time: 184 us; the launch traced here: 183 us
  matrix products  90.2 us (49%)
  waiting for transfers between devices  26 us (14%)
  loops' own time  23.8 us (13%)
  local copies, waits for them, and re-layouts  20 us (11%)
  starting transfers between devices  11.2 us (6%)
  between operations  6.83 us (4%)
  other arithmetic  4.89 us (3%)
    ppermute x10, waiting for transfers between devices, passed_along(): lax.ppermute(shard, axis, [(i, (i + by) % peers) for i in range(peers)])  26 us
    dot_general x12, matrix products, one_block(): jnp.einsum('uefjsgc,sehkf->ughckj', second, bra, preferred_element_type=j...  24.3 us
    another operation x2, loops' own time, per_device(): pieces = lax.map(one_block, starts)  23.8 us
    dot_general x12, matrix products, one_block(): jnp.einsum('uaebfj,sagcb->uefjsgc', first, ket_sites, preferred_element_t...  21.5 us
    ppermute x10, starting transfers between devices, passed_along(): lax.ppermute(shard, axis, [(i, (i + by) % peers) for i in range(peers)])  11.2 us
    dot_general x12, matrix products, one_block(): jnp.einsum('ughi,ughckj->jick', up_half, third, preferred_element_type=jn...  10.6 us
    dot_general x12, matrix products, polar_factor(): jnp.dot(iterate, gram, precision=lax.Precision.HIGHEST)  10.5 us
    dot_general x12, matrix products, polar_factor(): gram = jnp.dot(iterate.T, iterate, precision=lax.Precision.HIGHEST)  8.64 us
  transfers between devices with their start and end apart: 10, of which 6 were waited for; matrix products, arithmetic and copies ran while one was open for 48% of the time, Pallas kernels for 0%

commit v1 on v0

--- a/solution.py
+++ b/solution.py
@@ -3,10 +3,13 @@
 import jax
 import jax.numpy as jnp
 from jax import lax
+from jax.experimental import pallas as pl
+from jax.experimental.pallas import tpu as pltpu
 from jax.sharding import PartitionSpec as P
 
 NS_ITERS = 6
 STEPS = 2
+LANES = 128
 
 
 def passed_along(shard, axis, by):
@@ -27,6 +30,55 @@
     return tensor / jnp.sqrt(jnp.mean(tensor * tensor) + 1e-06)
 
 
+def edge_kernel(wd_ref, pm_ref, t_ref, qt_ref, o_ref, f_ref, g_ref):
+    n = qt_ref.shape[0]
+    dd = o_ref.shape[0]
+    ub = 8
+
+    def first_body(b, carry):
+        rows = wd_ref[pl.ds(pl.multiple_of(b * ub * dd, ub * dd), ub * dd), :]
+        for d in range(dd):
+            part = jnp.dot(rows, pm_ref[:, d * LANES:(d + 1) * LANES], preferred_element_type=jnp.float32)
+            f_ref[pl.ds(pl.multiple_of(b * ub, ub), ub), d] = part.astype(jnp.bfloat16).reshape(ub, dd, LANES)
+        return carry
+
+    lax.fori_loop(0, n // ub, first_body, 0)
+    t = t_ref[...]
+
+    def mid_body(h, carry):
+        x = jnp.concatenate([f_ref[h * 2 + k].reshape(dd * dd, LANES) for k in range(2)], axis=1)
+        g = jnp.dot(t, x, preferred_element_type=jnp.float32).astype(jnp.bfloat16)
+        for k in range(2):
+            at = pl.multiple_of((h * 2 + k) * dd, dd)
+            for r in range(dd):
+                g_ref[pl.ds(at, dd), r * LANES:(r + 1) * LANES] = g[r * dd:(r + 1) * dd, k * LANES:(k + 1) * LANES]
+        return carry
+
+    lax.fori_loop(0, n // 2, mid_body, 0)
+    qt = qt_ref[...]
+    for r in range(dd):
+        o_ref[r] = jnp.dot(qt, g_ref[:, r * LANES:(r + 1) * LANES], preferred_element_type=jnp.float32)
+
+
+def edge_contract(west, low_half, up_half, site):
+    n = west.shape[0]
+    dd = west.shape[1] // n
+    wd = west.reshape(n * dd, n)
+    pm = jnp.pad(low_half.reshape(n, dd, n), ((0, 0), (0, 0), (0, LANES - n))).reshape(n, dd * LANES)
+    qt = up_half.T
+    vmem = pltpu.MemorySpace.VMEM if hasattr(pltpu, "MemorySpace") else pltpu.VMEM
+    out = pl.pallas_call(
+        edge_kernel,
+        out_shape=jax.ShapeDtypeStruct((dd, n, LANES), jnp.float32),
+        scratch_shapes=[
+            pltpu.VMEM((n, dd, dd, LANES), jnp.bfloat16),
+            pltpu.VMEM((n * dd, dd * LANES), jnp.bfloat16),
+        ],
+        compiler_params=pltpu.CompilerParams(vmem_limit_bytes=48 * 1024 * 1024),
+    )(wd, pm, site, qt)
+    return jnp.transpose(out[:, :, :n], (1, 0, 2)).reshape(n, dd * n)
+
+
 def per_device(
     c_upper, edge_upper, edge_left, c_lower, edge_lower, site_ket, time_gate, quench_sites
 ):
@@ -42,13 +94,15 @@
     own_index = lax.axis_index("gx") * lax.axis_size("gy") + lax.axis_index("gy")
     chosen = jnp.any(quench_sites == own_index)
     bra = jnp.where(chosen, gated, ket_sites.astype(jnp.float32)).astype(jnp.bfloat16)
+    site = jnp.einsum(
+        "sagcb,sehkf->ckghbfae", ket_sites.astype(jnp.float32), bra.astype(jnp.float32),
+        precision=lax.Precision.HIGHEST,
+    ).reshape(double_bond * double_bond, double_bond * double_bond).astype(jnp.bfloat16)
     north_edge = edge_upper[0, 0]
     south_edge = edge_lower[0, 0]
     corner_up = c_upper[0, 0]
     west_edge = edge_left[0, 0]
     corner_low = c_lower[0, 0]
-    block = math.gcd(env_width, 16)
-    starts = jnp.arange(env_width // block, dtype=jnp.int32) * block
     for step in range(STEPS):
         upper = jnp.dot(corner_up, north_edge, preferred_element_type=jnp.float32).reshape(
             env_width * double_bond, env_width
@@ -59,29 +113,9 @@
         from_below = passed_along(upper.astype(jnp.bfloat16), "gy", -1).astype(upper.dtype)
         proj_below = polar_factor(lower + from_below)
         proj_above = passed_along(proj_below.astype(jnp.bfloat16), "gy", 1).astype(proj_below.dtype)
-        low_half = proj_below.astype(jnp.bfloat16).reshape(env_width, double_bond, env_width)
-        up_half = proj_above.astype(jnp.bfloat16).reshape(env_width, bond_dim, bond_dim, env_width)
-        west = west_edge.reshape(env_width, double_bond, env_width)
-
-        def one_block(start):
-            columns = lax.dynamic_slice_in_dim(low_half, start, block, 2)
-            first = jnp.einsum(
-                "ulw,wdj->uldj", west, columns, preferred_element_type=jnp.float32
-            ).astype(jnp.bfloat16)
-            first = first.reshape(env_width, bond_dim, bond_dim, bond_dim, bond_dim, block)
-            second = jnp.einsum(
-                "uaebfj,sagcb->uefjsgc", first, ket_sites, preferred_element_type=jnp.float32
-            ).astype(jnp.bfloat16)
-            third = jnp.einsum(
-                "uefjsgc,sehkf->ughckj", second, bra, preferred_element_type=jnp.float32
-            ).astype(jnp.bfloat16)
-            return jnp.einsum(
-                "ughi,ughckj->jick", up_half, third, preferred_element_type=jnp.float32
-            )
-
-        pieces = lax.map(one_block, starts)
-        edge_new = pieces.reshape(env_width, env_width, bond_dim, bond_dim)
-        edge_new = jnp.transpose(edge_new, (1, 2, 3, 0)).reshape(env_width, double_bond * env_width)
+        edge_new = edge_contract(
+            west_edge, proj_below.astype(jnp.bfloat16), proj_above.astype(jnp.bfloat16), site
+        )
         edge_new = unit_scaled(edge_new).astype(jnp.bfloat16)
         new_up = jnp.dot(proj_above.T, upper, precision=lax.Precision.HIGHEST)
         new_low = jnp.dot(proj_below.T, lower, precision=lax.Precision.HIGHEST)

time: 184 us -> 160 us (0.87)
  matrix products: 90.2 us -> 31.9 us
  local copies, waits for them, and re-layouts: 20 us -> 52.4 us
  Pallas kernels: 0 us -> 29.1 us
  loops' own time: 23.8 us -> 0 us
  waiting for transfers between devices: 26 us -> 19.7 us
  starting transfers between devices: 11.2 us -> 14.3 us
    dot_general x48 -> x1, matrix products: 62 us -> 4.26 us  [per_device(): jnp.einsum('sagcb,sehkf->ckghbfae', ket_sites.astype(jnp.float32), bra.as...]
    convert_element_type x0 -> x2, local copies, waits for them, and re-layouts: none -> 39 us  [per_device(): site = jnp.einsum('sagcb,sehkf->ckghbfae', ket_sites.astype(jnp.float32),...]
    pallas_call x0 -> x2, Pallas kernels: none -> 29.1 us  [edge_contract(): pl.pallas_call(edge_kernel, out_shape=jax.ShapeDtypeStruct((dd, n, LANES)...]
    another operation x2 -> x0, loops' own time: 23.8 us -> none  [per_device(): pieces = lax.map(one_block, starts)]
    dynamic_slice x12 -> x0, local copies, waits for them, and re-layouts: 7.04 us -> none  [per_device(): pieces = lax.map(one_block, starts)]
    ppermute x10, waiting for transfers between devices: 26 us -> 19.7 us  [passed_along(): lax.ppermute(shard, axis, [(i, (i + by) % peers) for i in range(peers)])]
    ppermute x10, starting transfers between devices: 11.2 us -> 14.3 us  [passed_along(): lax.ppermute(shard, axis, [(i, (i + by) % peers) for i in range(peers)])]
    while x8 -> x0, local copies, waits for them, and re-layouts: 2.44 us -> none  [per_device(): pieces = lax.map(one_block, starts)]
  transfers between devices with their start and end apart: 10 -> 10, of which waited for: 6 -> 5; matrix products, arithmetic and copies ran while one was open for 48% -> 39% of each run, Pallas kernels for 0% -> 18%
where the time goes in v1:
time: 160 us; the launch traced here: 159 us
  local copies, waits for them, and re-layouts  52.4 us (33%)
  matrix products  31.9 us (20%)
  Pallas kernels  29.1 us (18%)
  waiting for transfers between devices  19.7 us (12%)
  starting transfers between devices  14.3 us (9%)
  between operations  6.74 us (4%)
  other arithmetic  4.89 us (3%)
    convert_element_type x2, local copies, waits for them, and re-layouts, per_device(): site = jnp.einsum('sagcb,sehkf->ckghbfae', ket_sites.astype(jnp.float32),...  39 us
    pallas_call x2, Pallas kernels, edge_contract(): pl.pallas_call(edge_kernel, out_shape=jax.ShapeDtypeStruct((dd, n, LANES)...  29.1 us
    ppermute x10, waiting for transfers between devices, passed_along(): lax.ppermute(shard, axis, [(i, (i + by) % peers) for i in range(peers)])  19.7 us
    ppermute x10, starting transfers between devices, passed_along(): lax.ppermute(shard, axis, [(i, (i + by) % peers) for i in range(peers)])  14.3 us
    dot_general x12, matrix products, polar_factor(): jnp.dot(iterate, gram, precision=lax.Precision.HIGHEST)  10.5 us
    dot_general x12, matrix products, polar_factor(): gram = jnp.dot(iterate.T, iterate, precision=lax.Precision.HIGHEST)  8.65 us
    dot_general x1, matrix products, per_device(): jnp.einsum('sagcb,sehkf->ckghbfae', ket_sites.astype(jnp.float32), bra.as...  4.26 us
  transfers between devices with their start and end apart: 10, of which 5 were waited for; matrix products, arithmetic and copies ran while one was open for 39% of the time, Pallas kernels for 18%

profile of v1, /device:TPU:0, one launch (start us, length us, event | category | flops | bytes accessed | tf_op | source)
XLA Modules:
  0.0 159.0 jit_solution(8160665512874823087)
XLA Ops:
  0.7 0.9 copy-done
  1.6 0.9 fusion.19
  3.0 6.1 %collective-permute-start = (bf16[1536,96]{0,1:T(8,128)(2,1)S(1)}, bf16[1536,96]{0,1:T(8,128)(2,1)S(1)}, u32[]{:S(2)}, u32[]{:S(2)}) collective-permute-start(bf16[1536,96]{0,1:T(8,128)(2,1)S(1)} %copy.16), channel_id=1, source_target_pairs={{0,7},{1,0},{2,1},{3,2},{4,3},{5,4},{6,5},{7,6},{8,15},{9,8},{10,9... | collective-permute-start | bytes 884744 | tf_op jit(solution)/shard_map/ppermute | solution.py:17
  9.1 1.2 fusion.23
  11.0 0.6 compare_reduce_fusion
  11.8 0.9 fusion.12
  12.7 2.6 %collective-permute-done = bf16[1536,96]{0,1:T(8,128)(2,1)S(1)} collective-permute-done((bf16[1536,96]{0,1:T(8,128)(2,1)S(1)}, bf16[1536,96]{0,1:T(8,128)(2,1)S(1)}, u32[]{:S(2)}, u32[]{:S(2)}) %collective-permute-start) | collective-permute-done | bytes 294944 | tf_op jit(solution)/shard_map/ppermute | solution.py:17
  15.3 0.8 multiply_reduce_fusion.3
  16.8 0.7 fusion.28
  17.5 0.8 multiply_subtract_fusion.1
  18.3 0.6 fusion.37
  18.9 0.7 fusion.10
  19.6 0.6 fusion.38
  20.2 0.7 fusion.9
  21.0 0.6 fusion.39
  21.6 0.7 fusion.8
  22.3 0.6 fusion.40
  23.0 0.7 fusion.7
  23.7 0.6 fusion.41
  24.3 1.4 fusion.35
  25.8 0.3 collective-permute-start.2
  26.1 4.3 %fusion = bf16[4,4,4,4,4,4,4,4]{4,5,0,2,6,1,3,7:T(4,128)(2,1)} fusion(bf16[2,4,4,4,4,1,1,1]{4,0,7,6,5,3,2,1:T(2,128)(2,1)S(1)} %fusion.12, bf16[2,4,4,4,4,1,1,1]{4,3,2,1,0,7,6,5:T(4,128)(2,1)S(1)} %bitcast.113), kind=kOutput, calls=%fused_computation.1 | convolution fusion | flops 327680 | bytes 133120 | tf_op jit(solution)/shard_map/sagcb,sehkf->ckghbfae/dot_general | solution.py:97
  30.3 30.1 %copy.23 = bf16[4,4,4,4,4,4,4,4]{7,6,5,4,3,2,1,0:T(4,128)(2,1)} copy(bf16[4,4,4,4,4,4,4,4]{4,5,0,2,6,1,3,7:T(4,128)(2,1)} %fusion) | data formatting | bytes 262144 | tf_op jit(solution)/shard_map/convert_element_type | solution.py:100
  60.4 8.9 %convert_element_type.86.t_ref = bf16[256,256]{1,0:T(8,128)(2,1)S(1)} reshape(bf16[4,4,4,4,4,4,4,4]{7,6,5,4,3,2,1,0:T(4,128)(2,1)} %copy.23) | data formatting | bytes 262144 | tf_op jit(solution)/shard_map/convert_element_type | solution.py:100
  69.3 1.3 reshape_squeeze.6.wd_ref
  70.6 1.9 %copy.20 = bf16[1536,96]{1,0:T(8,128)(2,1)} copy(bf16[1536,96]{0,1:T(8,128)(2,1)} %get-tuple-element.5) | data formatting | bytes 589824 | tf_op jit(solution)/shard_map/convert_element_type | solution.py:115
  72.5 1.3 multiply_reduce_fusion.7
  74.5 1.1 pad.7
  75.7 1.1 multiply_reduce_fusion.6
  77.6 14.5 %shard_map.103 = f32[16,96,128]{2,1,0:T(8,128)S(1)} custom-call(bf16[1536,96]{1,0:T(8,128)(2,1)S(1)} %reshape_squeeze.6.wd_ref, bf16[96,2048]{1,0:T(8,128)(2,1)S(1)} %bitcast.104, bf16[256,256]{1,0:T(8,128)(2,1)S(1)} %convert_element_type.86.t_ref, bf16[96,1536]{1,0:T(8,128)(2,1)S(1)} %bitcast.107), custom_call_target="tpu_custom_call" | custom-call | tf_op jit(solution)/shard_map/pallas_call | solution.py:70
  92.1 0.8 multiply_reduce_fusion.1
  93.9 1.1 convert_element_type.89
  95.0 1.6 %collective-permute-start.7 = (bf16[96,1536]{1,0:T(8,128)(2,1)}, bf16[96,1536]{1,0:T(8,128)(2,1)}, u32[]{:S(2)}, u32[]{:S(2)}) collective-permute-start(bf16[96,1536]{1,0:T(8,128)(2,1)} %convert_element_type.89), channel_id=1, source_target_pairs={{0,8},{8,16},{16,24},{24,0},{1,9},{9,17},{17,25},{25,1},{2,10},{10... | collective-permute-start | bytes 884744 | tf_op jit(solution)/shard_map/ppermute | solution.py:17
  97.1 0.9 copy.18
  98.0 4.8 %collective-permute-start.4 = (bf16[1536,96]{0,1:T(8,128)(2,1)}, bf16[1536,96]{0,1:T(8,128)(2,1)}, u32[]{:S(2)}, u32[]{:S(2)}) collective-permute-start(bf16[1536,96]{0,1:T(8,128)(2,1)} %copy.18), channel_id=1, source_target_pairs={{0,7},{1,0},{2,1},{3,2},{4,3},{5,4},{6,5},{7,6},{8,15},{9,8},{10,9... | collective-permute-start | bytes 884744 | tf_op jit(solution)/shard_map/ppermute | solution.py:17
  102.8 0.3 collective-permute-start.1
  103.1 3.2 %collective-permute-done.1 = bf16[96,96]{1,0:T(8,128)(2,1)S(1)} collective-permute-done((bf16[96,96]{1,0:T(8,128)(2,1)S(1)}, bf16[96,96]{1,0:T(8,128)(2,1)S(1)}, u32[]{:S(2)}, u32[]{:S(2)}) %collective-permute-start.1) | collective-permute-done | bytes 18464 | tf_op jit(solution)/shard_map/ppermute | solution.py:17
  107.1 1.3 reshape.49.wd_ref
  108.4 1.2 collective-permute-done.4
  109.5 1.7 %multiply_reduce_fusion.2 = f32[]{:T(128)} fusion(f32[1536,96]{0,1:T(8,128)S(1)} %copy.19, bf16[1536,96]{0,1:T(8,128)(2,1)} %collective-permute-done.4), kind=kLoop, calls=%fused_computation.33 | loop fusion | flops 589823 | bytes 884740 | tf_op jit(solution)/shard_map/reduce_sum | solution.py:21
  111.9 1.8 %fusion.25 = f32[96,96]{1,0:T(8,128)S(1)} fusion(f32[1536,96]{0,1:T(8,128)S(1)} %copy.19, bf16[1536,96]{0,1:T(8,128)(2,1)} %collective-permute-done.4, f32[]{:T(128)S(6)} %sqrt.27), kind=kOutput, calls=%fused_computation.52 | convolution fusion | flops 170311680 | bytes 921604 | tf_op jit(solution)/shard_map/dot_general | solution.py:24
  113.7 1.8 %multiply_subtract_fusion = f32[1536,96]{0,1:T(8,128)S(1)} fusion(f32[96,96]{1,0:T(8,128)S(1)} %fusion.25, f32[]{:T(128)S(6)} %sqrt.27, f32[1536,96]{0,1:T(8,128)S(1)} %copy.19, bf16[1536,96]{0,1:T(8,128)(2,1)} %collective-permute-done.4), kind=kOutput, calls=%fused_computation.32 | convolution fusion | flops 171196416 | bytes 1511428 | tf_op jit(solution)/shard_map/dot_general | solution.py:25
  115.6 0.6 fusion.42
  116.2 0.7 fusion.5
  116.9 0.6 fusion.43
  117.5 0.7 fusion.4
  118.3 0.6 fusion.44
  118.9 0.7 fusion.3
  119.6 0.6 fusion.45
  120.2 0.7 fusion.2
  121.0 0.6 fusion.46
  121.6 0.7 fusion.36
  122.4 1.3 multiply_reduce_fusion.4
  124.7 0.3 collective-permute-start.9
  125.2 8.7 %collective-permute-done.5 = bf16[1536,96]{0,1:T(8,128)(2,1)S(1)} collective-permute-done((bf16[1536,96]{0,1:T(8,128)(2,1)S(1)}, bf16[1536,96]{0,1:T(8,128)(2,1)S(1)}, u32[]{:S(2)}, u32[]{:S(2)}) %collective-permute-start.5) | collective-permute-done | bytes 294944 | tf_op jit(solution)/shard_map/ppermute | solution.py:17
  133.9 14.5 %shard_map.104 = f32[16,96,128]{2,1,0:T(8,128)S(1)} custom-call(bf16[1536,96]{1,0:T(8,128)(2,1)S(1)} %reshape.49.wd_ref, bf16[96,2048]{1,0:T(8,128)(2,1)S(1)} %bitcast.105, bf16[256,256]{1,0:T(8,128)(2,1)S(1)} %convert_element_type.86.t_ref, bf16[96,1536]{1,0:T(8,128)(2,1)S(1)} %bitcast.106), custom_call_target="tpu_custom_call" | custom-call | tf_op jit(solution)/shard_map/pallas_call | solution.py:70
  148.4 0.8 multiply_reduce_fusion
  150.2 0.4 convert_element_type.92
  150.6 1.1 multiply_reduce_fusion.5
  152.4 0.7 collective-permute-start.6
  153.1 3.9 %collective-permute-done.6 = bf16[96,96]{1,0:T(8,128)(2,1)S(1)} collective-permute-done((bf16[96,96]{1,0:T(8,128)(2,1)S(1)}, bf16[96,96]{1,0:T(8,128)(2,1)S(1)}, u32[]{:S(2)}, u32[]{:S(2)}) %collective-permute-start.6) | collective-permute-done | bytes 18464 | tf_op jit(solution)/shard_map/ppermute | solution.py:17
  157.0 0.6 copy.45
  157.7 0.7 copy.46
  158.4 0.6 copy.47
  (40 shorter events, 3.6 us)
Async XLA Ops:
  0.6 1.0 copy-start
  0.6 10.2 %copy-start.2 = (bf16[1,1,2,256]{3,2,1,0:T(2,128)(2,1)S(1)}, bf16[1,1,2,256]{3,2,1,0:T(2,128)(2,1)}, u32[]{:S(2)}) copy-start(bf16[1,1,2,256]{3,2,1,0:T(2,128)(2,1)} %param.13) | copy-start | bytes 3076
  0.7 10.3 %copy-start.4 = (s32[4]{0:T(128)S(1)}, s32[4]{0:T(128)}, u32[]{:S(2)}) copy-start(s32[4]{0:T(128)} %param.15) | copy-start | bytes 52
  0.7 10.9 %copy-start.3 = (f32[2,2]{1,0:T(2,128)S(1)}, f32[2,2]{1,0:T(2,128)}, u32[]{:S(2)}) copy-start(f32[2,2]{1,0:T(2,128)} %param.14) | copy-start | bytes 52
  3.0 12.4 %collective-permute-start = (bf16[1536,96]{0,1:T(8,128)(2,1)S(1)}, bf16[1536,96]{0,1:T(8,128)(2,1)S(1)}, u32[]{:S(2)}, u32[]{:S(2)}) collective-permute-start(bf16[1536,96]{0,1:T(8,128)(2,1)S(1)} %copy.16), channel_id=1, source_target_pairs={{0,7},{1,0},{2,1},{3,2},{4,3},{5,4},{6,5},{7,6},{8,15},{9,8},{10,9... | collective-permute-start | bytes 884744 | tf_op jit(solution)/shard_map/ppermute | solution.py:17
  25.8 50.0 %collective-permute-start.2 = (bf16[1536,96]{0,1:T(8,128)(2,1)}, bf16[1536,96]{0,1:T(8,128)(2,1)S(1)}, u32[]{:S(2)}, u32[]{:S(2)}) collective-permute-start(bf16[1536,96]{0,1:T(8,128)(2,1)} %get-tuple-element.5), channel_id=1, source_target_pairs={{0,1},{1,2},{2,3},{3,4},{4,5},{5,6},{6,7},{7,0},{8,9},{9,10},{10,1... | collective-permute-start | bytes 884744 | tf_op jit(solution)/shard_map/ppermute | solution.py:17
  77.5 19.1 %collective-permute-start.3 = (bf16[96,96]{1,0:T(8,128)(2,1)S(1)}, bf16[96,96]{1,0:T(8,128)(2,1)S(1)}, u32[]{:S(2)}, u32[]{:S(2)}) collective-permute-start(bf16[96,96]{1,0:T(8,128)(2,1)S(1)} %divide_convert_fusion.4), channel_id=1, source_target_pairs={{0,8},{8,16},{16,24},{24,0},{1,9},{9,17},{17,25},{25,1},{2,10},{10... | collective-permute-start | bytes 55304 | tf_op jit(solution)/shard_map/ppermute | solution.py:17
  77.6 28.7 %copy-start.1 = (bf16[1,1,96,1536]{3,2,1,0:T(8,128)(2,1)S(1)}, bf16[1,1,96,1536]{3,2,1,0:T(8,128)(2,1)}, u32[]{:S(2)}) copy-start(bf16[1,1,96,1536]{3,2,1,0:T(8,128)(2,1)} %param.12) | copy-start | bytes 884740
  95.0 12.1 %collective-permute-start.7 = (bf16[96,1536]{1,0:T(8,128)(2,1)}, bf16[96,1536]{1,0:T(8,128)(2,1)}, u32[]{:S(2)}, u32[]{:S(2)}) collective-permute-start(bf16[96,1536]{1,0:T(8,128)(2,1)} %convert_element_type.89), channel_id=1, source_target_pairs={{0,8},{8,16},{16,24},{24,0},{1,9},{9,17},{17,25},{25,1},{2,10},{10... | collective-permute-start | bytes 884744 | tf_op jit(solution)/shard_map/ppermute | solution.py:17
  98.0 11.6 %collective-permute-start.4 = (bf16[1536,96]{0,1:T(8,128)(2,1)}, bf16[1536,96]{0,1:T(8,128)(2,1)}, u32[]{:S(2)}, u32[]{:S(2)}) collective-permute-start(bf16[1536,96]{0,1:T(8,128)(2,1)} %copy.18), channel_id=1, source_target_pairs={{0,7},{1,0},{2,1},{3,2},{4,3},{5,4},{6,5},{7,6},{8,15},{9,8},{10,9... | collective-permute-start | bytes 884744 | tf_op jit(solution)/shard_map/ppermute | solution.py:17
  102.8 3.5 %collective-permute-start.1 = (bf16[96,96]{1,0:T(8,128)(2,1)S(1)}, bf16[96,96]{1,0:T(8,128)(2,1)S(1)}, u32[]{:S(2)}, u32[]{:S(2)}) collective-permute-start(bf16[96,96]{1,0:T(8,128)(2,1)S(1)} %divide_convert_fusion.5), channel_id=1, source_target_pairs={{0,8},{8,16},{16,24},{24,0},{1,9},{9,17},{17,25},{25,1},{2,10},{10... | collective-permute-start | bytes 55304 | tf_op jit(solution)/shard_map/ppermute | solution.py:17
  122.3 11.6 %collective-permute-start.5 = (bf16[1536,96]{0,1:T(8,128)(2,1)S(1)}, bf16[1536,96]{0,1:T(8,128)(2,1)S(1)}, u32[]{:S(2)}, u32[]{:S(2)}) collective-permute-start(bf16[1536,96]{0,1:T(8,128)(2,1)S(1)} %get-tuple-element.9), channel_id=1, source_target_pairs={{0,1},{1,2},{2,3},{3,4},{4,5},{5,6},{6,7},{7,0},{8,9},{9,10},{10,1... | collective-permute-start | bytes 884744 | tf_op jit(solution)/shard_map/ppermute | solution.py:17
  124.7 28.5 %collective-permute-start.9 = (bf16[96,96]{1,0:T(8,128)(2,1)S(1)}, bf16[96,96]{1,0:T(8,128)(2,1)S(1)}, u32[]{:S(2)}, u32[]{:S(2)}) collective-permute-start(bf16[96,96]{1,0:T(8,128)(2,1)S(1)} %divide_convert_fusion.2), channel_id=1, source_target_pairs={{0,8},{8,16},{16,24},{24,0},{1,9},{9,17},{17,25},{25,1},{2,10},{10... | collective-permute-start | bytes 55304 | tf_op jit(solution)/shard_map/ppermute | solution.py:17
  150.6 6.5 %collective-permute-start.8 = (bf16[96,1536]{1,0:T(8,128)(2,1)S(1)}, bf16[96,1536]{1,0:T(8,128)(2,1)S(1)}, u32[]{:S(2)}, u32[]{:S(2)}) collective-permute-start(bf16[96,1536]{1,0:T(8,128)(2,1)S(1)} %convert_element_type.92), channel_id=1, source_target_pairs={{0,8},{8,16},{16,24},{24,0},{1,9},{9,17},{17,25},{25,1},{2,10},{10... | collective-permute-start | bytes 884744 | tf_op jit(solution)/shard_map/ppermute | solution.py:17
  152.4 4.6 %collective-permute-start.6 = (bf16[96,96]{1,0:T(8,128)(2,1)S(1)}, bf16[96,96]{1,0:T(8,128)(2,1)S(1)}, u32[]{:S(2)}, u32[]{:S(2)}) collective-permute-start(bf16[96,96]{1,0:T(8,128)(2,1)S(1)} %divide_convert_fusion.3), channel_id=1, source_target_pairs={{0,8},{8,16},{16,24},{24,0},{1,9},{9,17},{17,25},{25,1},{2,10},{10... | collective-permute-start | bytes 55304 | tf_op jit(solution)/shard_map/ppermute | solution.py:17

commit v2 on v1

--- a/solution.py
+++ b/solution.py
@@ -33,16 +33,11 @@
 def edge_kernel(wd_ref, pm_ref, t_ref, qt_ref, o_ref, f_ref, g_ref):
     n = qt_ref.shape[0]
     dd = o_ref.shape[0]
-    ub = 8
 
-    def first_body(b, carry):
-        rows = wd_ref[pl.ds(pl.multiple_of(b * ub * dd, ub * dd), ub * dd), :]
-        for d in range(dd):
-            part = jnp.dot(rows, pm_ref[:, d * LANES:(d + 1) * LANES], preferred_element_type=jnp.float32)
-            f_ref[pl.ds(pl.multiple_of(b * ub, ub), ub), d] = part.astype(jnp.bfloat16).reshape(ub, dd, LANES)
-        return carry
-
-    lax.fori_loop(0, n // ub, first_body, 0)
+    wd = wd_ref[...]
+    for d in range(dd):
+        part = jnp.dot(wd, pm_ref[:, d * LANES:(d + 1) * LANES], preferred_element_type=jnp.float32)
+        f_ref[:, d] = part.astype(jnp.bfloat16).reshape(n, dd, LANES)
     t = t_ref[...]
 
     def mid_body(h, carry):
@@ -79,6 +74,28 @@
     return jnp.transpose(out[:, :, :n], (1, 0, 2)).reshape(n, dd * n)
 
 
+def one_hot(rows, cols, row_key, col_key):
+    r = lax.broadcasted_iota(jnp.int32, (rows, cols), 0)
+    c = lax.broadcasted_iota(jnp.int32, (rows, cols), 1)
+    return (row_key(r) == col_key(c)).astype(jnp.float32)
+
+
+def double_layer(ket, bra):
+    q = ket.shape[1]
+    dd = q * q
+    size = dd * dd
+    ket_m = jnp.transpose(ket.astype(jnp.float32), (0, 3, 2, 4, 1)).reshape(ket.shape[0], dd, dd)
+    bra_m = jnp.transpose(bra.astype(jnp.float32), (0, 3, 2, 4, 1)).reshape(bra.shape[0], dd, dd)
+    k_row = one_hot(size, dd, lambda r: (r // (q * dd)) * q + (r // q) % q, lambda c: c)
+    b_row = one_hot(size, dd, lambda r: ((r // dd) % q) * q + r % q, lambda c: c)
+    k_col = one_hot(dd, size, lambda r: r, lambda c: (c // (q * dd)) * q + (c // q) % q)
+    b_col = one_hot(dd, size, lambda r: r, lambda c: ((c // dd) % q) * q + c % q)
+    hi = lax.Precision.HIGHEST
+    ket_wide = jnp.einsum("ra,sab,bc->src", k_row, ket_m, k_col, precision=hi)
+    bra_wide = jnp.einsum("ra,sab,bc->src", b_row, bra_m, b_col, precision=hi)
+    return jnp.sum(ket_wide * bra_wide, axis=0).astype(jnp.bfloat16)
+
+
 def per_device(
     c_upper, edge_upper, edge_left, c_lower, edge_lower, site_ket, time_gate, quench_sites
 ):
@@ -94,10 +111,7 @@
     own_index = lax.axis_index("gx") * lax.axis_size("gy") + lax.axis_index("gy")
     chosen = jnp.any(quench_sites == own_index)
     bra = jnp.where(chosen, gated, ket_sites.astype(jnp.float32)).astype(jnp.bfloat16)
-    site = jnp.einsum(
-        "sagcb,sehkf->ckghbfae", ket_sites.astype(jnp.float32), bra.astype(jnp.float32),
-        precision=lax.Precision.HIGHEST,
-    ).reshape(double_bond * double_bond, double_bond * double_bond).astype(jnp.bfloat16)
+    site = double_layer(ket_sites, bra)
     north_edge = edge_upper[0, 0]
     south_edge = edge_lower[0, 0]
     corner_up = c_upper[0, 0]

time: 160 us -> 112 us (0.70)
  local copies, waits for them, and re-layouts: 52.4 us -> 16.4 us
  matrix products: 31.9 us -> 26.9 us
  starting transfers between devices: 14.3 us -> 10.1 us
  Pallas kernels: 29.1 us -> 25.7 us
  waiting for transfers between devices: 19.7 us -> 22 us
    convert_element_type x2 -> x0, local copies, waits for them, and re-layouts: 39 us -> none  [per_device(): site = jnp.einsum('sagcb,sehkf->ckghbfae', ket_sites.astype(jnp.float32),...]
    ppermute x10, starting transfers between devices: 14.3 us -> 10.1 us  [passed_along(): lax.ppermute(shard, axis, [(i, (i + by) % peers) for i in range(peers)])]
    pallas_call x2, Pallas kernels: 29.1 us -> 25.7 us  [edge_contract(): pl.pallas_call(edge_kernel, out_shape=jax.ShapeDtypeStruct((dd, n, LANES)...]
    ppermute x10, waiting for transfers between devices: 19.7 us -> 22 us  [passed_along(): lax.ppermute(shard, axis, [(i, (i + by) % peers) for i in range(peers)])]
    unnamed x15 -> x25, local copies, waits for them, and re-layouts: 3.09 us -> 5.25 us
    dot_general x1 -> x4, matrix products: 4.26 us -> 2.45 us  [the longest x2 1.62 us: double_layer(): ket_wide = jnp.einsum('ra,sab,bc->src', k_row, ket_m, k_col, precision=hi)]
  transfers between devices with their start and end apart: 10 -> 10, of which waited for: 5 -> 5; matrix products, arithmetic and copies ran while one was open for 39% -> 19% of each run, Pallas kernels for 18% -> 23%
where the time goes in v2:
time: 112 us
  matrix products  26.9 us (24%)
  Pallas kernels  25.7 us (23%)
  waiting for transfers between devices  22 us (20%)
  local copies, waits for them, and re-layouts  16.4 us (15%)
  starting transfers between devices  10.1 us (9%)
  between operations  6.78 us (6%)
  other arithmetic  3.95 us (4%)
    pallas_call x2, Pallas kernels, edge_contract(): pl.pallas_call(edge_kernel, out_shape=jax.ShapeDtypeStruct((dd, n, LANES)...  25.7 us
    ppermute x10, waiting for transfers between devices, passed_along(): lax.ppermute(shard, axis, [(i, (i + by) % peers) for i in range(peers)])  22 us
    ppermute x10, starting transfers between devices, passed_along(): lax.ppermute(shard, axis, [(i, (i + by) % peers) for i in range(peers)])  10.1 us
    dot_general x12, matrix products, polar_factor(): jnp.dot(iterate, gram, precision=lax.Precision.HIGHEST)  9.48 us
    dot_general x12, matrix products, polar_factor(): gram = jnp.dot(iterate.T, iterate, precision=lax.Precision.HIGHEST)  7.54 us
    unnamed x25, local copies, waits for them, and re-layouts  5.25 us
    dot_general x2, matrix products, per_device(): new_low = jnp.dot(proj_below.T, lower, precision=lax.Precision.HIGHEST)  2.64 us
  transfers between devices with their start and end apart: 10, of which 5 were waited for; matrix products, arithmetic and copies ran while one was open for 19% of the time, Pallas kernels for 23%

profile of v2, /device:TPU:0, one launch (start us, length us, event | category | flops | bytes accessed | tf_op | source)
XLA Modules:
  0.0 111.9 jit_solution(12419984275112456388)
XLA Ops:
  0.6 1.0 copy-done
  1.6 0.9 fusion.19
  3.0 6.1 %collective-permute-start = (bf16[1536,96]{0,1:T(8,128)(2,1)S(1)}, bf16[1536,96]{0,1:T(8,128)(2,1)S(1)}, u32[]{:S(2)}, u32[]{:S(2)}) collective-permute-start(bf16[1536,96]{0,1:T(8,128)(2,1)S(1)} %copy.13), channel_id=1, source_target_pairs={{0,7},{1,0},{2,1},{3,2},{4,3},{5,4},{6,5},{7,6},{8,15},{9,8},{10,9... | collective-permute-start | bytes 884744 | tf_op jit(solution)/shard_map/ppermute | solution.py:17
  9.2 0.7 copy-done.8
  10.0 0.5 copy-done.7
  10.7 0.6 compare_reduce_fusion
  11.3 0.9 fusion.12
  13.0 0.6 copy-done.6
  13.9 0.4 fusion.32
  14.3 0.4 convolution_bitcast_fusion
  15.2 1.2 %fusion.72 = f32[2,256,256]{2,1,0:T(8,128)} fusion(f32[2,16,256]{2,1,0:T(8,128)S(1)} %convolution_bitcast_fusion, s32[256]{0:T(256)S(1)} %get-tuple-element.15, s32[256]{0:T(256)S(1)} %get-tuple-element.19, s32[256]{0:T(256)S(1)} %get-tuple-element.16, s32[256]{0:T(256)S(1)} %get-tuple-element.20, pred[256]{0:T(512)(128)(4,1)S(1)} %get-tuple-element.18, ...), kind=kOutput, calls=%fused_computation.122 | convolution fusion | flops 25231360 | bytes 561664 | tf_op jit(solution)/shard_map/ra,sab,bc->src/dot_general | solution.py:94
  16.4 0.8 multiply_reduce_fusion.3
  17.9 0.7 fusion.58
  18.6 0.8 multiply_subtract_fusion.1
  19.4 0.6 fusion.116
  20.0 0.7 fusion.9
  20.7 0.6 fusion.117
  21.3 0.7 fusion.8
  22.1 0.6 fusion.118
  22.7 0.7 fusion.7
  23.4 0.6 fusion.119
  24.0 0.7 fusion.6
  24.8 0.6 fusion.120
  25.4 1.4 %fusion.114 = (bf16[1536,96]{0,1:T(8,128)(2,1)}, f32[1536,96]{0,1:T(8,128)S(1)}) fusion(f32[1536,96]{0,1:T(8,128)S(1)} %fusion.6, f32[96,96]{1,0:T(8,128)S(1)} %fusion.120), kind=kOutput, calls=%fused_computation.176 | convolution fusion | flops 170459136 | bytes 1511424 | tf_op jit(solution)/shard_map/dot_general | solution.py:25
  26.9 0.4 fusion.10.t_ref
  27.3 1.3 %reshape_squeeze.6.wd_ref = bf16[1536,96]{1,0:T(8,128)(2,1)S(1)} reshape(bf16[1,1,96,1536]{3,2,1,0:T(8,128)(2,1)} %param.10) | data formatting | bytes 589824 | tf_op jit(solution)/shard_map/reshape;squeeze | solution.py:61
  28.6 1.9 %copy.17 = bf16[1536,96]{1,0:T(8,128)(2,1)} copy(bf16[1536,96]{0,1:T(8,128)(2,1)} %get-tuple-element.5) | data formatting | bytes 589824 | tf_op jit(solution)/shard_map/convert_element_type | solution.py:129
  30.5 1.3 %multiply_reduce_fusion.7 = (f32[]{:T(128)}, f32[96,96]{1,0:T(8,128)S(1)}) fusion(f32[1536,96]{0,1:T(8,128)S(1)} %get-tuple-element.6, f32[1536,96]{1,0:T(8,128)S(1)} %reshape.47), kind=kOutput, calls=%fused_computation.100 | convolution fusion | flops 169887744 | bytes 1216516 | tf_op jit(solution)/shard_map/dot_general | solution.py:135
  32.5 1.1 pad.7
  33.7 4.5 %collective-permute-done.2 = bf16[1536,96]{0,1:T(8,128)(2,1)S(1)} collective-permute-done((bf16[1536,96]{0,1:T(8,128)(2,1)}, bf16[1536,96]{0,1:T(8,128)(2,1)S(1)}, u32[]{:S(2)}, u32[]{:S(2)}) %collective-permute-start.2) | collective-permute-done | bytes 294944 | tf_op jit(solution)/shard_map/ppermute | solution.py:17
  38.2 1.1 multiply_reduce_fusion.6
  40.1 12.9 %shard_map.103 = f32[16,96,128]{2,1,0:T(8,128)S(1)} custom-call(bf16[1536,96]{1,0:T(8,128)(2,1)S(1)} %reshape_squeeze.6.wd_ref, bf16[96,2048]{1,0:T(8,128)(2,1)S(1)} %bitcast.118, bf16[256,256]{1,0:T(8,128)(2,1)S(1)} %fusion.10.t_ref, bf16[96,1536]{1,0:T(8,128)(2,1)S(1)} %bitcast.121), custom_call_target="tpu_custom_call" | custom-call | tf_op jit(solution)/shard_map/pallas_call | solution.py:65
  53.0 0.8 multiply_reduce_fusion.1
  54.7 1.1 convert_element_type.87
  55.8 1.6 %collective-permute-start.7 = (bf16[96,1536]{1,0:T(8,128)(2,1)}, bf16[96,1536]{1,0:T(8,128)(2,1)}, u32[]{:S(2)}, u32[]{:S(2)}) collective-permute-start(bf16[96,1536]{1,0:T(8,128)(2,1)} %convert_element_type.87), channel_id=1, source_target_pairs={{0,8},{8,16},{16,24},{24,0},{1,9},{9,17},{17,25},{25,1},{2,10},{10... | collective-permute-start | bytes 884744 | tf_op jit(solution)/shard_map/ppermute | solution.py:17
  57.9 0.9 copy.15
  58.8 0.8 collective-permute-start.4
  59.9 3.2 %collective-permute-done.1 = bf16[96,96]{1,0:T(8,128)(2,1)S(1)} collective-permute-done((bf16[96,96]{1,0:T(8,128)(2,1)S(1)}, bf16[96,96]{1,0:T(8,128)(2,1)S(1)}, u32[]{:S(2)}, u32[]{:S(2)}) %collective-permute-start.1) | collective-permute-done | bytes 18464 | tf_op jit(solution)/shard_map/ppermute | solution.py:17
  63.9 1.3 %reshape.55.wd_ref = bf16[1536,96]{1,0:T(8,128)(2,1)S(1)} reshape(bf16[96,1536]{1,0:T(8,128)(2,1)} %collective-permute-done.7) | data formatting | bytes 589824 | tf_op jit(solution)/shard_map/reshape | solution.py:61
  65.2 2.7 %collective-permute-done.4 = bf16[1536,96]{0,1:T(8,128)(2,1)S(1)} collective-permute-done((bf16[1536,96]{0,1:T(8,128)(2,1)}, bf16[1536,96]{0,1:T(8,128)(2,1)S(1)}, u32[]{:S(2)}, u32[]{:S(2)}) %collective-permute-start.4) | collective-permute-done | bytes 294944 | tf_op jit(solution)/shard_map/ppermute | solution.py:17
  67.9 0.8 multiply_reduce_fusion.2
  69.4 0.7 fusion.55
  70.0 0.8 multiply_subtract_fusion
  70.8 0.6 fusion.121
  71.5 0.7 fusion.4
  72.2 0.6 fusion.122
  72.8 0.7 fusion.3
  73.5 0.6 fusion.123
  74.2 0.7 fusion.2
  74.9 0.6 fusion.124
  75.5 0.7 fusion.1
  76.2 0.6 fusion.125
  76.9 0.7 fusion.115
  78.0 1.3 %multiply_reduce_fusion.4 = (f32[]{:T(128)}, f32[96,96]{1,0:T(8,128)S(1)}) fusion(f32[1536,96]{0,1:T(8,128)S(1)} %get-tuple-element.10, f32[1536,96]{1,0:T(8,128)S(1)} %copy-done.2), kind=kOutput, calls=%fused_computation.94 | convolution fusion | flops 169887744 | bytes 1216516 | tf_op jit(solution)/shard_map/dot_general | solution.py:135
  80.8 7.6 %collective-permute-done.5 = bf16[1536,96]{0,1:T(8,128)(2,1)S(1)} collective-permute-done((bf16[1536,96]{0,1:T(8,128)(2,1)S(1)}, bf16[1536,96]{0,1:T(8,128)(2,1)S(1)}, u32[]{:S(2)}, u32[]{:S(2)}) %collective-permute-start.5) | collective-permute-done | bytes 294944 | tf_op jit(solution)/shard_map/ppermute | solution.py:17
  88.4 12.9 %shard_map.104 = f32[16,96,128]{2,1,0:T(8,128)S(1)} custom-call(bf16[1536,96]{1,0:T(8,128)(2,1)S(1)} %reshape.55.wd_ref, bf16[96,2048]{1,0:T(8,128)(2,1)S(1)} %bitcast.119, bf16[256,256]{1,0:T(8,128)(2,1)S(1)} %fusion.10.t_ref, bf16[96,1536]{1,0:T(8,128)(2,1)S(1)} %bitcast.120), custom_call_target="tpu_custom_call" | custom-call | tf_op jit(solution)/shard_map/pallas_call | solution.py:65
  101.3 0.8 multiply_reduce_fusion
  103.1 0.4 convert_element_type.90
  103.5 1.1 multiply_reduce_fusion.5
  105.3 0.8 collective-permute-start.6
  106.1 3.8 %collective-permute-done.6 = bf16[96,96]{1,0:T(8,128)(2,1)S(1)} collective-permute-done((bf16[96,96]{1,0:T(8,128)(2,1)S(1)}, bf16[96,96]{1,0:T(8,128)(2,1)S(1)}, u32[]{:S(2)}, u32[]{:S(2)}) %collective-permute-start.6) | collective-permute-done | bytes 18464 | tf_op jit(solution)/shard_map/ppermute | solution.py:17
  109.9 0.6 copy.37
  110.5 0.7 copy.38
  111.2 0.6 copy.39
  (61 shorter events, 5.6 us)
Async XLA Ops:
  0.6 1.0 copy-start
  2.8 7.8 %copy-start.9 = (s32[4]{0:T(128)S(1)}, s32[4]{0:T(128)}, u32[]{:S(2)}) copy-start(s32[4]{0:T(128)} %param.15) | copy-start | bytes 52
  3.0 13.4 %collective-permute-start = (bf16[1536,96]{0,1:T(8,128)(2,1)S(1)}, bf16[1536,96]{0,1:T(8,128)(2,1)S(1)}, u32[]{:S(2)}, u32[]{:S(2)}) collective-permute-start(bf16[1536,96]{0,1:T(8,128)(2,1)S(1)} %copy.13), channel_id=1, source_target_pairs={{0,7},{1,0},{2,1},{3,2},{4,3},{5,4},{6,5},{7,6},{8,15},{9,8},{10,9... | collective-permute-start | bytes 884744 | tf_op jit(solution)/shard_map/ppermute | solution.py:17
  9.1 0.7 copy-start.8
  9.8 0.7 copy-start.7
  10.5 2.5 %copy-start.4 = (bf16[1,1,96,1536]{3,2,1,0:T(8,128)(2,1)S(1)}, bf16[1,1,96,1536]{3,2,1,0:T(8,128)(2,1)}, u32[]{:S(2)}) copy-start(bf16[1,1,96,1536]{3,2,1,0:T(8,128)(2,1)} %param.12) | copy-start | bytes 884740
  12.9 0.7 copy-start.6
  25.4 1.5 %copy-start.3 = (f32[2,256,256]{2,1,0:T(8,128)S(1)}, f32[2,256,256]{2,1,0:T(8,128)}, u32[]{:S(2)}) copy-start(f32[2,256,256]{2,1,0:T(8,128)} %fusion.72) | copy-start | bytes 1572868
  26.9 11.4 %collective-permute-start.2 = (bf16[1536,96]{0,1:T(8,128)(2,1)}, bf16[1536,96]{0,1:T(8,128)(2,1)S(1)}, u32[]{:S(2)}, u32[]{:S(2)}) collective-permute-start(bf16[1536,96]{0,1:T(8,128)(2,1)} %get-tuple-element.5), channel_id=1, source_target_pairs={{0,1},{1,2},{2,3},{3,4},{4,5},{5,6},{6,7},{7,0},{8,9},{9,10},{10,1... | collective-permute-start | bytes 884744 | tf_op jit(solution)/shard_map/ppermute | solution.py:17
  40.0 17.4 %collective-permute-start.3 = (bf16[96,96]{1,0:T(8,128)(2,1)S(1)}, bf16[96,96]{1,0:T(8,128)(2,1)S(1)}, u32[]{:S(2)}, u32[]{:S(2)}) collective-permute-start(bf16[96,96]{1,0:T(8,128)(2,1)S(1)} %divide_convert_fusion.4), channel_id=1, source_target_pairs={{0,8},{8,16},{16,24},{24,0},{1,9},{9,17},{17,25},{25,1},{2,10},{10... | collective-permute-start | bytes 55304 | tf_op jit(solution)/shard_map/ppermute | solution.py:17
  55.8 8.1 %collective-permute-start.7 = (bf16[96,1536]{1,0:T(8,128)(2,1)}, bf16[96,1536]{1,0:T(8,128)(2,1)}, u32[]{:S(2)}, u32[]{:S(2)}) collective-permute-start(bf16[96,1536]{1,0:T(8,128)(2,1)} %convert_element_type.87), channel_id=1, source_target_pairs={{0,8},{8,16},{16,24},{24,0},{1,9},{9,17},{17,25},{25,1},{2,10},{10... | collective-permute-start | bytes 884744 | tf_op jit(solution)/shard_map/ppermute | solution.py:17
  57.9 5.2 %copy-start.5 = (bf16[1,1,96,1536]{3,2,1,0:T(8,128)(2,1)S(1)}, bf16[1,1,96,1536]{3,2,1,0:T(8,128)(2,1)}, u32[]{:S(2)}) copy-start(bf16[1,1,96,1536]{3,2,1,0:T(8,128)(2,1)} %param.12) | copy-start | bytes 884740
  58.8 9.1 %collective-permute-start.4 = (bf16[1536,96]{0,1:T(8,128)(2,1)}, bf16[1536,96]{0,1:T(8,128)(2,1)S(1)}, u32[]{:S(2)}, u32[]{:S(2)}) collective-permute-start(bf16[1536,96]{0,1:T(8,128)(2,1)} %copy.15), channel_id=1, source_target_pairs={{0,7},{1,0},{2,1},{3,2},{4,3},{5,4},{6,5},{7,6},{8,15},{9,8},{10,9... | collective-permute-start | bytes 884744 | tf_op jit(solution)/shard_map/ppermute | solution.py:17
  59.6 3.5 %collective-permute-start.1 = (bf16[96,96]{1,0:T(8,128)(2,1)S(1)}, bf16[96,96]{1,0:T(8,128)(2,1)S(1)}, u32[]{:S(2)}, u32[]{:S(2)}) collective-permute-start(bf16[96,96]{1,0:T(8,128)(2,1)S(1)} %divide_convert_fusion.5), channel_id=1, source_target_pairs={{0,8},{8,16},{16,24},{24,0},{1,9},{9,17},{17,25},{25,1},{2,10},{10... | collective-permute-start | bytes 55304 | tf_op jit(solution)/shard_map/ppermute | solution.py:17
  63.6 1.6 %copy-start.1 = (f32[1536,96]{1,0:T(8,128)}, f32[1536,96]{1,0:T(8,128)S(1)}, u32[]{:S(2)}) copy-start(f32[1536,96]{1,0:T(8,128)S(1)} %reshape.49) | copy-start | bytes 1769476
  76.9 1.1 %copy-start.2 = (f32[1536,96]{1,0:T(8,128)S(1)}, f32[1536,96]{1,0:T(8,128)}, u32[]{:S(2)}) copy-start(f32[1536,96]{1,0:T(8,128)} %copy-done.1) | copy-start | bytes 1769476
  77.6 10.8 %collective-permute-start.5 = (bf16[1536,96]{0,1:T(8,128)(2,1)S(1)}, bf16[1536,96]{0,1:T(8,128)(2,1)S(1)}, u32[]{:S(2)}, u32[]{:S(2)}) collective-permute-start(bf16[1536,96]{0,1:T(8,128)(2,1)S(1)} %get-tuple-element.9), channel_id=1, source_target_pairs={{0,1},{1,2},{2,3},{3,4},{4,5},{5,6},{6,7},{7,0},{8,9},{9,10},{10,1... | collective-permute-start | bytes 884744 | tf_op jit(solution)/shard_map/ppermute | solution.py:17
  80.3 25.8 %collective-permute-start.9 = (bf16[96,96]{1,0:T(8,128)(2,1)S(1)}, bf16[96,96]{1,0:T(8,128)(2,1)S(1)}, u32[]{:S(2)}, u32[]{:S(2)}) collective-permute-start(bf16[96,96]{1,0:T(8,128)(2,1)S(1)} %divide_convert_fusion.2), channel_id=1, source_target_pairs={{0,8},{8,16},{16,24},{24,0},{1,9},{9,17},{17,25},{25,1},{2,10},{10... | collective-permute-start | bytes 55304 | tf_op jit(solution)/shard_map/ppermute | solution.py:17
  103.5 6.5 %collective-permute-start.8 = (bf16[96,1536]{1,0:T(8,128)(2,1)S(1)}, bf16[96,1536]{1,0:T(8,128)(2,1)S(1)}, u32[]{:S(2)}, u32[]{:S(2)}) collective-permute-start(bf16[96,1536]{1,0:T(8,128)(2,1)S(1)} %convert_element_type.90), channel_id=1, source_target_pairs={{0,8},{8,16},{16,24},{24,0},{1,9},{9,17},{17,25},{25,1},{2,10},{10... | collective-permute-start | bytes 884744 | tf_op jit(solution)/shard_map/ppermute | solution.py:17
  105.3 4.6 %collective-permute-start.6 = (bf16[96,96]{1,0:T(8,128)(2,1)S(1)}, bf16[96,96]{1,0:T(8,128)(2,1)S(1)}, u32[]{:S(2)}, u32[]{:S(2)}) collective-permute-start(bf16[96,96]{1,0:T(8,128)(2,1)S(1)} %divide_convert_fusion.3), channel_id=1, source_target_pairs={{0,8},{8,16},{16,24},{24,0},{1,9},{9,17},{17,25},{25,1},{2,10},{10... | collective-permute-start | bytes 55304 | tf_op jit(solution)/shard_map/ppermute | solution.py:17
